TPU v7x, 256 devices: a whole 4x4x8 slice. The times are simulated.
256 devices in a mesh: dp: 128 (over y, z, x_lo, core), rows: 2 (over x_hi).
Axes of the slice: x: 4 (x_hi: 2, x_lo: 2; x = x_hi * 2 + x_lo), y: 4, z: 8, core: 2. Of those that a mesh axis runs over, the one named last changes fastest.
Arguments:
- features: bfloat16 [128, 32, 32, 768], P('dp', 'rows'), may hold values from -24 to 24
- bucket: int32 [128], P('dp'), may hold values from 0 to 16, as said below
- kernel: float32 [7, 7, 768], replicated, may hold values from -0.875 to 0.875
- up_weight: bfloat16 [768, 2816], P('dp'), may hold values from -0.21875 to 0.21875
- down_weight: bfloat16 [2816, 768], P('dp'), may hold values from -0.109375 to 0.109375
- cotangent: bfloat16 [128, 32, 32, 768], P('dp', 'rows'), may hold values from -6 to 6
Outputs:
- block_out: bfloat16 [128, 32, 32, 768], P('dp', 'rows')
- feature_grad: bfloat16 [128, 32, 32, 768], P('dp', 'rows')
- up_grad: float32 [768, 2816], P('dp')
- down_grad: float32 [2816, 768], P('dp')
- kernel_grad: float32 [7, 7, 768], replicated
Inputs may be any that keep to these rules, and one draw needn't show every extreme that they name: `bucket`: both ends of the range occur in every draw.
All inputs are finite; a program needn't handle non-finite values.
Results may differ from a plain program's by a relative error of at most 0.0075.
Values may be sent and summed in bfloat16 or wider, within the bound.
No kernel may reach another device: no remote copies, remote signals or barrier semaphores. Data moves between devices by JAX's collectives and lax.ppermute only.
A program may use at most 128 MiB of HBM per device.

v0:
```python
import jax
import jax.numpy as jnp
from jax import lax
from jax.sharding import PartitionSpec as P

INV_ROOT_TWO = 0.7071067811865476
INV_ROOT_TAU = 0.3989422804014327
EPSILON = 1e-06


def in_order(tiles, dim):
    tiles = jnp.moveaxis(tiles, 0, dim)
    lengths = tiles.shape
    return tiles.reshape(*lengths[:dim], lengths[dim] * lengths[dim + 1], *lengths[dim + 2 :])


def one_gather(arrays, axis, dims):
    vector = jnp.concatenate([a.reshape(-1) for a in arrays])
    lines, at, finished = (lax.all_gather(vector, axis), 0, [])
    for a, dim in zip(arrays, dims):
        tiles = lines[:, at : at + a.size].reshape(-1, *a.shape)
        finished.append(in_order(tiles, dim))
        at += a.size
    return tuple(finished)


def padded_2(block, sides, width):
    for axis, dim in sides:
        count = lax.axis_size(axis)
        forward = [(i, i + 1) for i in range(count - 1)]
        backward = [(target, source) for source, target in forward]
        low = lax.ppermute(
            lax.slice_in_dim(block, block.shape[dim] - width, None, axis=dim), axis, forward
        )
        high = lax.ppermute(lax.slice_in_dim(block, 0, width, axis=dim), axis, backward)
        block = jnp.concatenate([low, block, high], axis=dim)
    return block


def cut_along(array, dim, devices):
    before, after = (array.shape[:dim], array.shape[dim + 1 :])
    return jnp.moveaxis(array.reshape(*before, devices, -1, *after), dim, 0)


def sum_in_tiles(array, axis, dim):
    devices = lax.axis_size(axis)
    tiles = cut_along(array, dim, devices)
    lines = tiles.reshape(devices, -1)
    rows = max(16, -(-lines.shape[1] // 1024) * 8)
    lines = jnp.pad(lines, ((0, 0), (0, rows * 128 - lines.shape[1]))).reshape(-1, 128)
    own = lax.psum_scatter(lines, axis, scatter_dimension=0, tiled=True)
    return own.reshape(-1)[: tiles[0].size].reshape(tiles.shape[1:])


def gelu_parts(pre_act):
    normal_cdf = 0.5 * (1.0 + lax.erf(pre_act * INV_ROOT_TWO))
    density = jnp.exp(-0.5 * pre_act * pre_act) * INV_ROOT_TAU
    return (pre_act * normal_cdf, normal_cdf + pre_act * density)


def depthwise(padded, kernel, out_rows, out_cols, flipped):
    span = kernel.shape[0]
    result = jnp.zeros(padded.shape[:-3] + (out_rows, out_cols, padded.shape[-1]), jnp.float32)
    for offset_row in range(span):
        for offset_col in range(span):
            start_row = span - 1 - offset_row if flipped else offset_row
            start_col = span - 1 - offset_col if flipped else offset_col
            result = (
                result
                + kernel[offset_row, offset_col]
                * padded[..., start_row : start_row + out_rows, start_col : start_col + out_cols, :]
            )
    return result


def kernel_terms(grad_conv, padded, span):
    reduce_axes = tuple(range(grad_conv.ndim - 1))
    rows_out = grad_conv.shape[-3]
    cols_out = grad_conv.shape[-2]
    kernel_rows = []
    for offset_row in range(span):
        kernel_row = []
        for offset_col in range(span):
            window = padded[
                ..., offset_row : offset_row + rows_out, offset_col : offset_col + cols_out, :
            ]
            kernel_row.append(jnp.sum(grad_conv * window, axis=reduce_axes))
        kernel_rows.append(jnp.stack(kernel_row))
    return jnp.stack(kernel_rows)


def layer_norm(convolved):
    centered = convolved - jnp.mean(convolved, axis=-1, keepdims=True)
    inv_std = lax.rsqrt(jnp.mean(centered * centered, axis=-1, keepdims=True) + EPSILON)
    return (centered * inv_std, inv_std)


def norm_backward(grad_norm, unit_norm, inv_std):
    first_mean = jnp.mean(grad_norm, axis=-1, keepdims=True)
    second_mean = jnp.mean(grad_norm * unit_norm, axis=-1, keepdims=True)
    return inv_std * (grad_norm - first_mean - unit_norm * second_mean)


def pointwise(tokens, cot_rows, up_full, down_full):
    pre_act = jnp.dot(tokens, up_full, preferred_element_type=jnp.float32)
    hidden, derivative = gelu_parts(pre_act)
    activation = hidden.astype(jnp.bfloat16)
    branch = jnp.dot(activation, down_full, preferred_element_type=jnp.float32)
    grad_act = lax.dot_general(
        cot_rows, down_full, (((1,), (1,)), ((), ())), preferred_element_type=jnp.float32
    )
    grad_pre = (grad_act * derivative).astype(jnp.bfloat16)
    grad_norm = lax.dot_general(
        grad_pre, up_full, (((1,), (1,)), ((), ())), preferred_element_type=jnp.float32
    )
    return (activation, branch, grad_pre, grad_norm)


def on_device(features, bucket, kernel, up_weight, down_weight, cotangent):
    images, strip_rows, canvas_cols, channels = features.shape
    rows_count = lax.axis_size("rows")
    row_index = lax.axis_index("rows")
    canvas_rows = strip_rows * rows_count
    area_cells = canvas_rows * canvas_cols // 2
    reach = kernel.shape[0] // 2
    grad_scale = 1.0 / (images * lax.axis_size("dp"))
    heights = canvas_rows // 2 + bucket
    widths = jnp.minimum(canvas_cols, area_cells // heights)
    row_ids = row_index * strip_rows + lax.iota(jnp.int32, strip_rows)
    col_ids = lax.iota(jnp.int32, canvas_cols)
    inside = (row_ids[None, :, None] < heights[:, None, None]) & (
        col_ids[None, None, :] < widths[:, None, None]
    )
    inside_cells = inside[..., None]
    masked = jnp.where(inside_cells, features, jnp.zeros((), features.dtype))
    masked_cot = jnp.where(inside_cells, cotangent, jnp.zeros((), cotangent.dtype))
    up_full, down_full = one_gather((up_weight, down_weight), "dp", (0, 0))
    rimmed = padded_2(masked, (("rows", 1),), reach)
    padded = jnp.pad(rimmed, ((0, 0), (0, 0), (reach, reach), (0, 0)))
    convolved = jnp.where(
        inside_cells, depthwise(padded, kernel, strip_rows, canvas_cols, False), 0.0
    )
    unit_norm, inv_std = layer_norm(convolved)
    normed = unit_norm.astype(jnp.bfloat16)
    tokens = normed.reshape(images * strip_rows * canvas_cols, channels)
    cot_rows = masked_cot.reshape(images * strip_rows * canvas_cols, channels)
    activation, branch_rows, grad_pre, grad_rows = pointwise(tokens, cot_rows, up_full, down_full)
    branch = branch_rows.reshape(features.shape)
    grad_norm = grad_rows.reshape(features.shape)
    block_out = (masked + branch).astype(jnp.bfloat16)
    grad_conv = jnp.where(inside_cells, norm_backward(grad_norm, unit_norm, inv_std), 0.0)
    kernel_grad = lax.psum(
        kernel_terms(grad_conv, padded, kernel.shape[0]) * grad_scale, ("dp", "rows")
    )
    grad_rimmed = padded_2(grad_conv.astype(jnp.bfloat16), (("rows", 1),), reach).astype(
        grad_conv.dtype
    )
    grad_padded = jnp.pad(grad_rimmed, ((0, 0), (0, 0), (reach, reach), (0, 0)))
    feature_grad = jnp.where(
        inside_cells,
        masked_cot + depthwise(grad_padded, kernel, strip_rows, canvas_cols, True),
        0.0,
    ).astype(jnp.bfloat16)
    columns = tokens
    up_piece = sum_in_tiles(
        lax.dot_general(
            columns, grad_pre, (((0,), (0,)), ((), ())), preferred_element_type=jnp.float32
        )
        * grad_scale,
        ("dp", "rows"),
        0,
    )
    columns = activation
    down_piece = lax.psum_scatter(
        lax.dot_general(
            columns, cot_rows, (((0,), (0,)), ((), ())), preferred_element_type=jnp.float32
        )
        * grad_scale,
        ("dp", "rows"),
        scatter_dimension=0,
        tiled=True,
    )
    up_grad, down_grad = tuple(
        (
            part.astype(jnp.float32)
            for part in one_gather(
                (up_piece.astype(jnp.bfloat16), down_piece.astype(jnp.bfloat16)), "rows", (0, 0)
            )
        )
    )
    return (block_out, feature_grad, up_grad, down_grad, kernel_grad)


def solution(mesh):
    placed = (
        P("dp", "rows", None, None),
        P("dp"),
        P(),
        P("dp", None),
        P("dp", None),
        P("dp", "rows", None, None),
    )
    return jax.shard_map(
        on_device,
        mesh=mesh,
        in_specs=placed,
        out_specs=(
            P("dp", "rows", None, None),
            P("dp", "rows", None, None),
            P("dp", None),
            P("dp", None),
            P(),
        ),
        check_vma=False,
    )
```

profile of v0, /device:TPU:2, one launch (start us, length us, event | category | flops | bytes accessed | tf_op | source)
XLA Modules:
  0.0 591.3 jit_solution(8514478073993602004)
XLA Ops:
  7.2 0.9 reshape.354
  8.1 0.8 reshape.355
  8.9 0.6 pad_maximum_fusion.2
  10.4 2.5 broadcast_select_fusion
  12.9 4.0 collective-permute-start
  16.9 1.3 collective-permute-start.1
  18.2 0.2 slice_reduce_fusion.48
  18.4 0.1 slice_reduce_fusion.46
  18.5 0.2 slice_reduce_fusion.47
  18.7 1.3 collective-permute-done
  20.0 5.6 collective-permute-done.1
  25.6 0.6 fusion.203
  26.2 16.5 %fusion.210 = (f32[16,32]{1,0:T(8,128)S(1)}, f32[1,16,32,768]{3,2,1,0:T(8,128)S(1)}) fusion(bf16[1,22,38,768]{3,2,1,0:T(8,128)(2,1)S(1)} %fusion.203, f32[768]{0:T(1024)S(1)} %get-tuple-element.104, f32[768]{0:T(1024)S(1)} %get-tuple-element.105, f32[768]{0:T(1024)S(1)} %get-tuple-element.58, bf16[1,3,32,768]{3,2,1,0:T(8,128)(2,1)S(1)} %collective-permute-done.1, ...), kind=kLoop, calls=%fused_computation.453 | loop fusion | flops 60554752 | bytes 35837440 | tf_op jit(solution)/shard_map/reduce_sum | solution.py:93
  42.8 0.3 multiply_reduce_fusion.1
  43.1 1.1 fusion.204
  44.2 190.0 %all-gather.5.cloned.1.call-done = bf16[4325376]{0:T(1024)(128)(2,1)} async-done(((bf16[33792]{0:T(1024)(128)(2,1)}), bf16[4325376]{0:T(1024)(128)(2,1)}) %all-gather.5.cloned.1.call-update) | async-done | bytes 8650768 | tf_op jit(solution)/shard_map/all_gather | solution.py:19
  234.2 13.5 %reshape.363 = bf16[128,33792]{1,0:T(8,128)(2,1)} reshape(bf16[4325376]{0:T(1024)(128)(2,1)} %all-gather.5.cloned.1.call-done) | data formatting | bytes 17301504 | tf_op jit(solution)/shard_map/all_gather | solution.py:19
  247.7 5.8 fusion.212
  253.5 9.8 %reshape.368 = bf16[2816,768,1]{1,0,2:T(8,128)(2,1)} reshape(bf16[128,16896]{1,0:T(8,128)(2,1)} %get-tuple-element.111) | data formatting | bytes 8650752 | tf_op jit(solution)/shard_map/reshape;reshape | solution.py:14
  263.3 9.8 %reshape_reshape.12 = bf16[2816,768]{1,0:T(8,128)(2,1)} reshape(bf16[128,16896]{1,0:T(8,128)(2,1)} %get-tuple-element.111) | data formatting | bytes 8650752 | tf_op jit(solution)/shard_map/reshape;reshape | solution.py:14
  273.1 9.0 %reshape_reshape.11 = bf16[768,2816]{1,0:T(8,128)(2,1)} reshape(bf16[128,16896]{1,0:T(8,128)(2,1)} %get-tuple-element.112) | data formatting | bytes 8650752 | tf_op jit(solution)/shard_map/reshape;reshape | solution.py:14
  282.1 6.1 %multiply_convert_fusion = (bf16[512,2816]{1,0:T(8,128)(2,1)}, f32[512,2816]{1,0:T(8,128)S(1)}) fusion(bf16[512,768]{1,0:T(8,128)(2,1)} %bitcast.46, bf16[768,2816]{1,0:T(8,128)(2,1)} %reshape_reshape.11), kind=kOutput, calls=%fused_computation.51 | convolution fusion | flops 2221801472 | bytes 13762560 | tf_op jit(solution)/shard_map/dot_general | solution.py:105
  288.2 3.7 fusion.5
  291.9 3.6 fusion.215
  295.6 1.9 multiply_reduce_fusion
  297.6 4.9 fusion.102
  302.5 1.3 fusion.38
  303.8 4.0 fusion.81
  307.8 5.8 convolution_multiply_fusion.1
  313.6 1.2 fusion.99
  315.9 0.7 broadcast_multiply_fusion
  316.6 4.2 collective-permute-start.2
  320.8 1.3 collective-permute-start.3
  322.1 10.0 %reshape_reshape.13 = f32[256,8448]{1,0:T(8,128)} reshape(f32[768,2816]{1,0:T(8,128)} %convolution_multiply_fusion.1) | data formatting | bytes 17301504 | tf_op jit(solution)/shard_map/reshape;reshape | solution.py:48
  332.1 8.4 %pad.14 = f32[256,9216]{1,0:T(8,128)} pad(f32[256,8448]{1,0:T(8,128)} %reshape_reshape.13, f32[]{:T(128)} %constant.43.clone.1), padding=0_0x0_768 | pad | bytes 18087940 | tf_op jit(solution)/shard_map/jit(_pad)/pad | solution.py:50
  340.5 10.0 %reshape.359 = f32[18432,128]{1,0:T(8,128)} reshape(f32[256,9216]{1,0:T(8,128)} %pad.14) | data formatting | bytes 18874368 | tf_op jit(solution)/shard_map/reshape | solution.py:50
  350.6 7.7 %convolution_multiply_fusion = f32[2816,768]{1,0:T(8,128)} fusion(bf16[512,2816]{1,0:T(8,128)(2,1)} %get-tuple-element.122, bf16[512,768]{1,0:T(8,128)(2,1)S(1)} %bitcast.45), kind=kOutput, calls=%fused_computation.43 | convolution fusion | flops 2216755200 | bytes 12320768 | tf_op jit(solution)/shard_map/dot_general | solution.py:175
  358.2 194.9 %all-reduce.10 = (bf16[2816,768]{1,0:T(8,128)(2,1)}, bf16[18432,128]{1,0:T(8,128)(2,1)}) all-reduce(f32[2816,768]{1,0:T(8,128)} %convolution_multiply_fusion, f32[18432,128]{1,0:T(8,128)} %reshape.359), channel_id=5, replica_groups=mesh['dp'=128,'rows'=2] {'dp','rows'}, use_global_device_ids=true, to_apply=%region_5.6.clone | all-reduce | flops 4521984 | bytes 27131904
  553.1 0.8 dynamic-slice_convert_fusion
  553.9 0.7 fusion.209
  554.7 6.5 %all-gather.2 = bf16[2,1,16896]{2,1,0:T(2,128)(2,1)S(1)} all-gather(bf16[1,1,16896]{2,1,0:T(2,128)(2,1)S(1)} %reshape.365), channel_id=3, replica_groups=mesh['dp'=128,'rows'=2] {'rows'}, dimensions={0}, use_global_device_ids=true | all-gather | bytes 101376 | tf_op jit(solution)/shard_map/all_gather | solution.py:19
  561.3 6.4 %fusion.103 = bf16[1,16,32,768]{3,2,1,0:T(8,128)(2,1)} fusion(bf16[1,16,32,768]{3,2,1,0:T(8,128)(2,1)S(1)} %copy-done.1, bf16[16,32,2816]{2,1,0:T(8,128)(2,1)} %bitcast.48, bf16[2816,768,1]{1,0,2:T(8,128)(2,1)} %reshape.368), kind=kOutput, calls=%fused_computation.251 | convolution fusion | flops 2215772160 | bytes 8781824 | tf_op jit(solution)/shard_map/dot_general | solution.py:108
  567.7 0.7 reshape.362
  568.4 0.7 reshape.361
  569.2 0.2 maximum_convert_fusion
  569.3 0.9 copy-done.4
  570.3 12.6 %fusion.194 = bf16[1,16,32,768]{3,2,1,0:T(8,128)(2,1)} fusion(f32[1,22,32,768]{3,2,1,0:T(8,128)S(1)} %maximum_convert_fusion, f32[768]{0:T(1024)S(1)} %get-tuple-element.104, f32[768]{0:T(1024)S(1)} %get-tuple-element.105, f32[768]{0:T(1024)S(1)} %get-tuple-element.58, f32[768]{0:T(1024)S(1)} %get-tuple-element.59, f32[768]{0:T(1024)S(1)} %get-tuple-element.60, ...), kind=kLoop, calls=%fused_computation.342 | loop fusion | flops 40108032 | bytes 14948352 | tf_op jit(solution)/shard_map/convert_element_type | solution.py:163
  582.9 1.6 copy.26
  (127 shorter events, 1.2 us)
Async XLA Ops:
  7.2 227.1 %all-gather.5.cloned.1.call-start = ((), (), s32[]{:S(2)}) async-start(), calls=%async_computation.1 | async-start | bytes 8718336 | tf_op jit(solution)/shard_map/all_gather | solution.py:19
  9.6 573.3 %all-reduce.9.cloned.1.call-start = ((), (), s32[]{:S(2)}) async-start(), calls=%async_computation | async-start | bytes 344064 | tf_op jit(solution)/shard_map/psum | solution.py:152
  10.4 7.8 %copy-start.10 = (f32[7,7,768]{2,1,0:T(8,128)S(1)}, f32[7,7,768]{2,1,0:T(8,128)}, u32[]{:S(2)}) copy-start(f32[7,7,768]{2,1,0:T(8,128)} %param.8) | copy-start | bytes 451588
  12.9 13.4 %copy-start = (bf16[1,16,32,768]{3,2,1,0:T(8,128)(2,1)}, bf16[1,16,32,768]{3,2,1,0:T(8,128)(2,1)S(1)}, u32[]{:S(2)}) copy-start(bf16[1,16,32,768]{3,2,1,0:T(8,128)(2,1)S(1)} %get-tuple-element.121) | copy-start | bytes 2359300
  12.9 7.1 %collective-permute-start = (bf16[1,3,32,768]{3,2,1,0:T(8,128)(2,1)S(1)}, bf16[1,3,32,768]{3,2,1,0:T(8,128)(2,1)S(1)}, u32[]{:S(2)}, u32[]{:S(2)}) collective-permute-start(bf16[1,3,32,768]{3,2,1,0:T(8,128)(2,1)S(1)} %get-tuple-element.116), channel_id=1, source_target_pairs={{0,1},{2,3},{4,5},{6,7},{8,9},{10,11},{12,13},{14,15},{16,17},{18,... | collective-permute-start | bytes 442376 | tf_op jit(solution)/shard_map/ppermute | solution.py:32
  16.9 8.7 %collective-permute-start.1 = (bf16[1,3,32,768]{3,2,1,0:T(8,128)(2,1)S(1)}, bf16[1,3,32,768]{3,2,1,0:T(8,128)(2,1)S(1)}, u32[]{:S(2)}, u32[]{:S(2)}) collective-permute-start(bf16[1,3,32,768]{3,2,1,0:T(8,128)(2,1)S(1)} %get-tuple-element.117), channel_id=1, source_target_pairs={{1,0},{3,2},{5,4},{7,6},{9,8},{11,10},{13,12},{15,14},{17,16},{19,... | collective-permute-start | bytes 442376 | tf_op jit(solution)/shard_map/ppermute | solution.py:35
  18.7 24.1 %copy-start.11 = (f32[768]{0:T(1024)}, f32[768]{0:T(1024)S(1)}, u32[]{:S(2)}) copy-start(f32[768]{0:T(1024)S(1)} %get-tuple-element.91) | copy-start | bytes 9220
  18.7 24.1 %copy-start.13 = (f32[768]{0:T(1024)}, f32[768]{0:T(1024)S(1)}, u32[]{:S(2)}) copy-start(f32[768]{0:T(1024)S(1)} %get-tuple-element.92) | copy-start | bytes 9220
  18.7 24.1 %copy-start.15 = (f32[768]{0:T(1024)}, f32[768]{0:T(1024)S(1)}, u32[]{:S(2)}) copy-start(f32[768]{0:T(1024)S(1)} %get-tuple-element.93) | copy-start | bytes 9220
  18.7 24.1 %copy-start.17 = (f32[768]{0:T(1024)}, f32[768]{0:T(1024)S(1)}, u32[]{:S(2)}) copy-start(f32[768]{0:T(1024)S(1)} %get-tuple-element.94) | copy-start | bytes 9220
  282.1 6.1 %copy-start.3 = (bf16[2816,768]{1,0:T(8,128)(2,1)S(1)}, bf16[2816,768]{1,0:T(8,128)(2,1)}, u32[]{:S(2)}) copy-start(bf16[2816,768]{1,0:T(8,128)(2,1)} %reshape_reshape.12) | copy-start | bytes 12976132
  282.1 6.1 %copy-start.5 = (bf16[1,16,32,768]{3,2,1,0:T(8,128)(2,1)S(1)}, bf16[1,16,32,768]{3,2,1,0:T(8,128)(2,1)}, u32[]{:S(2)}) copy-start(bf16[1,16,32,768]{3,2,1,0:T(8,128)(2,1)} %get-tuple-element.120) | copy-start | bytes 2359300
  282.1 9.8 %slice-start = ((s8[4325376]{0:T(1024)(128)(4,1)}), s8[4194304]{0:T(1024)(128)(4,1)S(1)}, s32[]{:S(2)}) async-start(s8[4325376]{0:T(1024)(128)(4,1)} %bitcast.42), calls=%async_computation.2 | async-start | bytes 8388608
  288.2 3.7 slice-start.1
  291.9 3.6 copy-start.8
  295.6 2.0 copy-start.2
  303.8 4.1 copy-start.7
  303.8 4.1 copy-start.9
  307.8 5.8 copy-start.1
  316.6 252.5 %collective-permute-start.2 = (bf16[1,3,32,768]{3,2,1,0:T(8,128)(2,1)S(1)}, bf16[1,3,32,768]{3,2,1,0:T(8,128)(2,1)S(1)}, u32[]{:S(2)}, u32[]{:S(2)}) collective-permute-start(bf16[1,3,32,768]{3,2,1,0:T(8,128)(2,1)S(1)} %get-tuple-element.114), channel_id=1, source_target_pairs={{0,1},{2,3},{4,5},{6,7},{8,9},{10,11},{12,13},{14,15},{16,17},{18,... | collective-permute-start | bytes 442376 | tf_op jit(solution)/shard_map/ppermute | solution.py:32
  320.8 248.3 %collective-permute-start.3 = (bf16[1,3,32,768]{3,2,1,0:T(8,128)(2,1)S(1)}, bf16[1,3,32,768]{3,2,1,0:T(8,128)(2,1)S(1)}, u32[]{:S(2)}, u32[]{:S(2)}) collective-permute-start(bf16[1,3,32,768]{3,2,1,0:T(8,128)(2,1)S(1)} %get-tuple-element.115), channel_id=1, source_target_pairs={{1,0},{3,2},{5,4},{7,6},{9,8},{11,10},{13,12},{15,14},{17,16},{19,... | collective-permute-start | bytes 442376 | tf_op jit(solution)/shard_map/ppermute | solution.py:35
  340.5 10.1 %copy-start.6 = (bf16[1,16,32,768]{3,2,1,0:T(8,128)(2,1)S(1)}, bf16[1,16,32,768]{3,2,1,0:T(8,128)(2,1)}, u32[]{:S(2)}) copy-start(bf16[1,16,32,768]{3,2,1,0:T(8,128)(2,1)} %get-tuple-element.120) | copy-start | bytes 2359300
  569.1 1.1 copy-start.4
  569.1 1.1 copy-start.12
  569.1 1.1 copy-start.14
  569.1 1.1 copy-start.16
  569.1 1.1 copy-start.18
Sparse Core Ops, SparseCore 0:
  10.4 223.7 all-gather.4
  316.7 243.3 all-reduce.8
where the time goes:
time: 594 us; the launch traced here: 591 us
  blocking collectives  201 us (34%)
  waiting for transfers between devices  197 us (33%)
  local copies, waits for them, and re-layouts  84.7 us (14%)
  other arithmetic  48.7 us (8%)
  matrix products  33.2 us (6%)
  between operations  15.6 us (3%)
  starting transfers between devices  10.9 us (2%)
    unnamed x1, blocking collectives  195 us
    all_gather x1, waiting for transfers between devices, one_gather(): lines, at, finished = (lax.all_gather(vector, axis), 0, [])  190 us
    another operation x3, local copies, waits for them, and re-layouts, in_order(): tiles.reshape(*lengths[:dim], lengths[dim] * lengths[dim + 1], *lengths[d...  28.6 us
    reduce_sum x1, other arithmetic, layer_norm(): centered = convolved - jnp.mean(convolved, axis=-1, keepdims=True)  16.5 us
    all_gather x1, local copies, waits for them, and re-layouts, one_gather(): lines, at, finished = (lax.all_gather(vector, axis), 0, [])  13.5 us
    convert_element_type x1, other arithmetic, on_device(): feature_grad = jnp.where(inside_cells, masked_cot + depthwise(grad_padded...  12.6 us
  transfers between devices with their start and end apart: 6, of which 3 were waited for; matrix products, arithmetic and copies ran while one was open for 14% of the time, Pallas kernels for 0%

commit v1 on v0

v1 whole, which is shorter than its diff:
```python
import jax
import jax.numpy as jnp
from jax import lax
from jax.sharding import Mesh
from jax.sharding import PartitionSpec as P

INV_ROOT_TWO = 0.7071067811865476
INV_ROOT_TAU = 0.3989422804014327
EPSILON = 1e-06

AXES = ("y", "z", "xl", "c", "rows")
SIZES = (4, 8, 2, 2, 2)
DP = AXES[:4]
SIZE = dict(zip(AXES, SIZES))


def ring_gather(x, axis):
    n = SIZE[axis]
    me = lax.axis_index(axis)
    m = x.shape[0]
    out = jnp.zeros((n * m,) + x.shape[1:], x.dtype)
    out = lax.dynamic_update_slice_in_dim(out, x, me * m, 0)
    right = n // 2
    left = n - 1 - right
    cur = x
    for s in range(1, right + 1):
        cur = lax.ppermute(cur, axis, [(i, (i + 1) % n) for i in range(n)])
        out = lax.dynamic_update_slice_in_dim(out, cur, ((me - s) % n) * m, 0)
    cur = x
    for s in range(1, left + 1):
        cur = lax.ppermute(cur, axis, [(i, (i - 1) % n) for i in range(n)])
        out = lax.dynamic_update_slice_in_dim(out, cur, ((me + s) % n) * m, 0)
    return out


def ring_scatter(x, axis, wire):
    n = SIZE[axis]
    me = lax.axis_index(axis)
    m = x.shape[0] // n

    def block(j):
        return lax.dynamic_slice_in_dim(x, (j % n) * m, m, 0)

    if n == 2:
        got = lax.ppermute(block(me + 1).astype(wire), axis, [(0, 1), (1, 0)])
        return block(me) + got.astype(jnp.float32)
    half = x.shape[1] // 2
    acc_r = block(me - 1)[:, :half]
    acc_l = block(me + 1)[:, half:]
    for s in range(1, n):
        got_r = lax.ppermute(acc_r.astype(wire), axis, [(i, (i + 1) % n) for i in range(n)])
        got_l = lax.ppermute(acc_l.astype(wire), axis, [(i, (i - 1) % n) for i in range(n)])
        j_r, j_l = (me - s - 1, me + s + 1) if s < n - 1 else (me, me)
        acc_r = got_r.astype(jnp.float32) + block(j_r)[:, :half]
        acc_l = got_l.astype(jnp.float32) + block(j_l)[:, half:]
    return jnp.concatenate([acc_r, acc_l], axis=1)


def gather_weight(shard):
    rows = shard.shape[0]
    for axis in ("c", "xl", "y", "z"):
        shard = ring_gather(shard, axis)
    shard = shard.reshape(SIZE["z"], SIZE["y"], -1, shard.shape[1]).transpose(1, 0, 2, 3)
    return shard.reshape(-1, shard.shape[3])


def reduce_weight_grad(term):
    order = ("c", "z", "y", "xl")
    n = term.shape[0]
    tiles = term.reshape(*SIZES[:4], n // 128, term.shape[1])
    tiles = tiles.transpose([DP.index(a) for a in order] + [4, 5]).reshape(n, -1)
    for axis in order:
        tiles = ring_scatter(tiles, axis, jnp.bfloat16)
    return tiles + lax.ppermute(tiles, "rows", [(0, 1), (1, 0)])


def padded_2(block, sides, width):
    for axis, dim in sides:
        count = lax.axis_size(axis)
        forward = [(i, i + 1) for i in range(count - 1)]
        backward = [(target, source) for source, target in forward]
        low = lax.ppermute(
            lax.slice_in_dim(block, block.shape[dim] - width, None, axis=dim), axis, forward
        )
        high = lax.ppermute(lax.slice_in_dim(block, 0, width, axis=dim), axis, backward)
        block = jnp.concatenate([low, block, high], axis=dim)
    return block


def gelu_parts(pre_act):
    normal_cdf = 0.5 * (1.0 + lax.erf(pre_act * INV_ROOT_TWO))
    density = jnp.exp(-0.5 * pre_act * pre_act) * INV_ROOT_TAU
    return (pre_act * normal_cdf, normal_cdf + pre_act * density)


def depthwise(padded, kernel, out_rows, out_cols, flipped):
    span = kernel.shape[0]
    result = jnp.zeros(padded.shape[:-3] + (out_rows, out_cols, padded.shape[-1]), jnp.float32)
    for offset_row in range(span):
        for offset_col in range(span):
            start_row = span - 1 - offset_row if flipped else offset_row
            start_col = span - 1 - offset_col if flipped else offset_col
            result = (
                result
                + kernel[offset_row, offset_col]
                * padded[..., start_row : start_row + out_rows, start_col : start_col + out_cols, :]
            )
    return result


def kernel_terms(grad_conv, padded, span):
    reduce_axes = tuple(range(grad_conv.ndim - 1))
    rows_out = grad_conv.shape[-3]
    cols_out = grad_conv.shape[-2]
    kernel_rows = []
    for offset_row in range(span):
        kernel_row = []
        for offset_col in range(span):
            window = padded[
                ..., offset_row : offset_row + rows_out, offset_col : offset_col + cols_out, :
            ]
            kernel_row.append(jnp.sum(grad_conv * window, axis=reduce_axes))
        kernel_rows.append(jnp.stack(kernel_row))
    return jnp.stack(kernel_rows)


def layer_norm(convolved):
    centered = convolved - jnp.mean(convolved, axis=-1, keepdims=True)
    inv_std = lax.rsqrt(jnp.mean(centered * centered, axis=-1, keepdims=True) + EPSILON)
    return (centered * inv_std, inv_std)


def norm_backward(grad_norm, unit_norm, inv_std):
    first_mean = jnp.mean(grad_norm, axis=-1, keepdims=True)
    second_mean = jnp.mean(grad_norm * unit_norm, axis=-1, keepdims=True)
    return inv_std * (grad_norm - first_mean - unit_norm * second_mean)


def on_device(features, bucket, kernel, up_weight, down_weight, cotangent):
    images, strip_rows, canvas_cols, channels = features.shape
    rows_count = lax.axis_size("rows")
    row_index = lax.axis_index("rows")
    canvas_rows = strip_rows * rows_count
    area_cells = canvas_rows * canvas_cols // 2
    reach = kernel.shape[0] // 2
    grad_scale = 1.0 / (images * lax.axis_size(DP))
    heights = canvas_rows // 2 + bucket
    widths = jnp.minimum(canvas_cols, area_cells // heights)
    row_ids = row_index * strip_rows + lax.iota(jnp.int32, strip_rows)
    col_ids = lax.iota(jnp.int32, canvas_cols)
    inside = (row_ids[None, :, None] < heights[:, None, None]) & (
        col_ids[None, None, :] < widths[:, None, None]
    )
    inside_cells = inside[..., None]
    masked = jnp.where(inside_cells, features, jnp.zeros((), features.dtype))
    masked_cot = jnp.where(inside_cells, cotangent, jnp.zeros((), cotangent.dtype))
    up_full = gather_weight(up_weight)
    down_full = gather_weight(down_weight)
    rimmed = padded_2(masked, (("rows", 1),), reach)
    padded = jnp.pad(rimmed, ((0, 0), (0, 0), (reach, reach), (0, 0)))
    convolved = jnp.where(
        inside_cells, depthwise(padded, kernel, strip_rows, canvas_cols, False), 0.0
    )
    unit_norm, inv_std = layer_norm(convolved)
    normed = unit_norm.astype(jnp.bfloat16)
    tokens = normed.reshape(images * strip_rows * canvas_cols, channels)
    cot_rows = masked_cot.reshape(images * strip_rows * canvas_cols, channels)

    pre_act = jnp.dot(tokens, up_full, preferred_element_type=jnp.float32)
    hidden, derivative = gelu_parts(pre_act)
    activation = hidden.astype(jnp.bfloat16)
    down_term = lax.dot_general(
        activation, cot_rows, (((0,), (0,)), ((), ())), preferred_element_type=jnp.float32
    )
    down_grad = reduce_weight_grad(down_term * grad_scale)
    branch = jnp.dot(activation, down_full, preferred_element_type=jnp.float32)
    grad_act = lax.dot_general(
        cot_rows, down_full, (((1,), (1,)), ((), ())), preferred_element_type=jnp.float32
    )
    grad_pre = (grad_act * derivative).astype(jnp.bfloat16)
    up_term = lax.dot_general(
        tokens, grad_pre, (((0,), (0,)), ((), ())), preferred_element_type=jnp.float32
    )
    up_grad = reduce_weight_grad(up_term * grad_scale)
    grad_rows = lax.dot_general(
        grad_pre, up_full, (((1,), (1,)), ((), ())), preferred_element_type=jnp.float32
    )

    branch = branch.reshape(features.shape)
    grad_norm = grad_rows.reshape(features.shape)
    block_out = (masked + branch).astype(jnp.bfloat16)
    grad_conv = jnp.where(inside_cells, norm_backward(grad_norm, unit_norm, inv_std), 0.0)
    kernel_grad = lax.psum(
        kernel_terms(grad_conv, padded, kernel.shape[0]) * grad_scale, AXES
    )
    grad_rimmed = padded_2(grad_conv.astype(jnp.bfloat16), (("rows", 1),), reach).astype(
        grad_conv.dtype
    )
    grad_padded = jnp.pad(grad_rimmed, ((0, 0), (0, 0), (reach, reach), (0, 0)))
    feature_grad = jnp.where(
        inside_cells,
        masked_cot + depthwise(grad_padded, kernel, strip_rows, canvas_cols, True),
        0.0,
    ).astype(jnp.bfloat16)
    return (block_out, feature_grad, up_grad, down_grad, kernel_grad)


def solution(mesh):
    torus = Mesh(mesh.devices.reshape(SIZES), AXES)
    strips = P(DP, "rows", None, None)
    return jax.shard_map(
        on_device,
        mesh=torus,
        in_specs=(strips, P(DP), P(), P(DP, None), P(DP, None), strips),
        out_specs=(strips, strips, P(DP, None), P(DP, None), P()),
        check_vma=False,
    )
```

time: 594 us -> 485 us (0.82); the launches traced: 591 us -> 476 us
  blocking collectives: 201 us -> 0 us
  starting transfers between devices: 10.9 us -> 99.9 us
  local copies, waits for them, and re-layouts: 84.7 us -> 77.1 us
    unnamed x1 -> x0, blocking collectives: 195 us -> none
    all_gather x1 -> x0, waiting for transfers between devices: 190 us -> none  [one_gather(): lines, at, finished = (lax.all_gather(vector, axis), 0, [])]
    ppermute x0 -> x70, waiting for transfers between devices: none -> 116 us  [the longest x16 81.6 us: ring_gather(): cur = lax.ppermute(cur, axis, [(i, (i + 1) % n) for i in range(n)])]
    ppermute x0 -> x70, starting transfers between devices: none -> 87.3 us  [the longest x20 37.2 us: ring_scatter(): lax.ppermute(acc_l.astype(wire), axis, [(i, (i - 1) % n) for i in range(n)])]
    psum x1, waiting for transfers between devices: 0.01 us -> 79.2 us  [on_device(): lax.psum(kernel_terms(grad_conv, padded, kernel.shape[0]) * grad_scale, A...]
    another operation x4 -> x0, local copies, waits for them, and re-layouts: 38.6 us -> none  [the longest x3 28.6 us: in_order(): tiles.reshape(*lengths[:dim], lengths[dim] * lengths[dim + 1], *lengths[d...]
    reshape x4, local copies, waits for them, and re-layouts: 11.8 us -> 38.8 us  [the longest x2 19.5 us: reduce_weight_grad(): tiles.transpose([DP.index(a) for a in order] + [4, 5]).reshape(n, -1)]
    transpose x0 -> x4, local copies, waits for them, and re-layouts: none -> 19.7 us  [the longest x2 19.1 us: reduce_weight_grad(): tiles.transpose([DP.index(a) for a in order] + [4, 5]).reshape(n, -1)]
  transfers between devices with their start and end apart: 6 -> 75, of which waited for: 3 -> 35; matrix products, arithmetic and copies ran while one was open for 14% -> 20% of each run, Pallas kernels for 0% -> 0%
where the time goes in v1:
time: 485 us; the launch traced here: 476 us
  waiting for transfers between devices  197 us (41%)
  starting transfers between devices  99.9 us (21%)
  local copies, waits for them, and re-layouts  77.1 us (16%)
  other arithmetic  52.5 us (11%)
  matrix products  31.2 us (6%)
  between operations  18.2 us (4%)
    ppermute x16, waiting for transfers between devices, ring_gather(): cur = lax.ppermute(cur, axis, [(i, (i + 1) % n) for i in range(n)])  81.6 us
    psum x1, waiting for transfers between devices, on_device(): lax.psum(kernel_terms(grad_conv, padded, kernel.shape[0]) * grad_scale, A...  79.2 us
    ppermute x20, starting transfers between devices, ring_scatter(): lax.ppermute(acc_l.astype(wire), axis, [(i, (i - 1) % n) for i in range(n)])  37.2 us
    ppermute x20, waiting for transfers between devices, ring_scatter(): lax.ppermute(acc_r.astype(wire), axis, [(i, (i + 1) % n) for i in range(n)])  29.3 us
    ppermute x8, starting transfers between devices, ring_gather(): cur = lax.ppermute(cur, axis, [(i, (i - 1) % n) for i in range(n)])  19.6 us
    reshape x2, local copies, waits for them, and re-layouts, reduce_weight_grad(): tiles.transpose([DP.index(a) for a in order] + [4, 5]).reshape(n, -1)  19.5 us
    reshape x2, local copies, waits for them, and re-layouts, reduce_weight_grad(): tiles = term.reshape(*SIZES[:4], n // 128, term.shape[1])  19.3 us
    transpose x2, local copies, waits for them, and re-layouts, reduce_weight_grad(): tiles.transpose([DP.index(a) for a in order] + [4, 5]).reshape(n, -1)  19.1 us
  transfers between devices with their start and end apart: 75, of which 35 were waited for; matrix products, arithmetic and copies ran while one was open for 20% of the time, Pallas kernels for 0%

profile of v1, /device:TPU:2, one launch (start us, length us, event | category | flops | bytes accessed | tf_op | source)
XLA Modules:
  0.0 476.0 jit_solution(8201712412584277900)
XLA Ops:
  8.6 2.5 broadcast_select_fusion
  11.1 4.2 collective-permute-start
  25.4 3.1 collective-permute-start.18
  29.2 3.3 collective-permute-start.6
  34.2 16.3 %fusion.275 = (f32[16,32]{1,0:T(8,128)S(1)}, f32[1,16,32,768]{3,2,1,0:T(8,128)S(1)}) fusion(bf16[1,22,38,768]{3,2,1,0:T(8,128)(2,1)S(1)} %fusion.203, f32[768]{0:T(1024)S(1)} %copy-done.82, f32[768]{0:T(1024)S(1)} %copy-done.84, f32[768]{0:T(1024)S(1)} %get-tuple-element.58, bf16[1,3,32,768]{3,2,1,0:T(8,128)(2,1)S(1)} %collective-permute-done.1, ...), kind=kLoop, calls=%fused_computation.611 | loop fusion | flops 60554752 | bytes 35837440 | tf_op jit(solution)/shard_map/reduce_sum | solution.py:128
  52.9 4.1 collective-permute-done.17
  62.3 2.5 collective-permute-start.11
  66.9 10.2 %collective-permute-done.19 = bf16[352,768]{1,0:T(8,128)(2,1)S(1)} collective-permute-done((bf16[352,768]{1,0:T(8,128)(2,1)S(1)}, bf16[352,768]{1,0:T(8,128)(2,1)S(1)}, u32[]{:S(2)}, u32[]{:S(2)}) %collective-permute-start.19) | collective-permute-done | bytes 540704 | tf_op jit(solution)/shard_map/ppermute | solution.py:27
  77.3 11.3 %collective-permute-done.7 = bf16[96,2816]{1,0:T(8,128)(2,1)S(1)} collective-permute-done((bf16[96,2816]{1,0:T(8,128)(2,1)S(1)}, bf16[96,2816]{1,0:T(8,128)(2,1)S(1)}, u32[]{:S(2)}, u32[]{:S(2)}) %collective-permute-start.7) | collective-permute-done | bytes 540704 | tf_op jit(solution)/shard_map/ppermute | solution.py:27
  89.0 3.7 collective-permute-start.12
  93.9 6.4 %collective-permute-done.20 = bf16[352,768]{1,0:T(8,128)(2,1)S(1)} collective-permute-done((bf16[352,768]{1,0:T(8,128)(2,1)S(1)}, bf16[352,768]{1,0:T(8,128)(2,1)S(1)}, u32[]{:S(2)}, u32[]{:S(2)}) %collective-permute-start.20) | collective-permute-done | bytes 540704 | tf_op jit(solution)/shard_map/ppermute | solution.py:27
  100.3 11.5 %collective-permute-done.8 = bf16[96,2816]{1,0:T(8,128)(2,1)S(1)} collective-permute-done((bf16[96,2816]{1,0:T(8,128)(2,1)S(1)}, bf16[96,2816]{1,0:T(8,128)(2,1)S(1)}, u32[]{:S(2)}, u32[]{:S(2)}) %collective-permute-start.8) | collective-permute-done | bytes 540704 | tf_op jit(solution)/shard_map/ppermute | solution.py:27
  111.9 3.3 collective-permute-start.13
  116.1 7.4 %collective-permute-done.21 = bf16[352,768]{1,0:T(8,128)(2,1)S(1)} collective-permute-done((bf16[352,768]{1,0:T(8,128)(2,1)S(1)}, bf16[352,768]{1,0:T(8,128)(2,1)S(1)}, u32[]{:S(2)}, u32[]{:S(2)}) %collective-permute-start.21) | collective-permute-done | bytes 540704 | tf_op jit(solution)/shard_map/ppermute | solution.py:27
  123.5 11.5 %collective-permute-done.9 = bf16[96,2816]{1,0:T(8,128)(2,1)S(1)} collective-permute-done((bf16[96,2816]{1,0:T(8,128)(2,1)S(1)}, bf16[96,2816]{1,0:T(8,128)(2,1)S(1)}, u32[]{:S(2)}, u32[]{:S(2)}) %collective-permute-start.9) | collective-permute-done | bytes 540704 | tf_op jit(solution)/shard_map/ppermute | solution.py:27
  135.1 11.5 %collective-permute-done.22 = bf16[352,768]{1,0:T(8,128)(2,1)S(1)} collective-permute-done((bf16[352,768]{1,0:T(8,128)(2,1)S(1)}, bf16[352,768]{1,0:T(8,128)(2,1)S(1)}, u32[]{:S(2)}, u32[]{:S(2)}) %collective-permute-start.22) | collective-permute-done | bytes 540704 | tf_op jit(solution)/shard_map/ppermute | solution.py:27
  147.1 7.1 %collective-permute-done.10 = bf16[96,2816]{1,0:T(8,128)(2,1)S(1)} collective-permute-done((bf16[96,2816]{1,0:T(8,128)(2,1)S(1)}, bf16[96,2816]{1,0:T(8,128)(2,1)S(1)}, u32[]{:S(2)}, u32[]{:S(2)}) %collective-permute-start.10) | collective-permute-done | bytes 540704 | tf_op jit(solution)/shard_map/ppermute | solution.py:27
  154.8 4.5 multiply_convert_fusion
  159.3 3.7 fusion.5
  163.0 3.6 fusion.281
  168.7 4.7 fusion.102
  174.7 4.0 fusion.81
  178.8 6.0 %convolution_multiply_fusion.1 = f32[768,2816]{1,0:T(8,128)} fusion(bf16[512,768]{1,0:T(8,128)(2,1)S(1)} %bitcast.64, bf16[512,2816]{1,0:T(8,128)(2,1)S(1)} %copy-done.11), kind=kOutput, calls=%fused_computation.44 | convolution fusion | flops 2216755200 | bytes 12320768 | tf_op jit(solution)/shard_map/dot_general | solution.py:181
  186.7 9.8 %reshape.362 = f32[4,8,2,2,6,2816]{5,4,3,2,1,0:T(8,128)} reshape(f32[768,2816]{1,0:T(8,128)} %convolution_multiply_fusion.1) | data formatting | bytes 17301504 | tf_op jit(solution)/shard_map/reshape | solution.py:70
  196.4 10.3 %copy.17 = f32[2,8,4,2,6,2816]{5,4,3,2,1,0:T(8,128)} copy(f32[2,8,4,2,6,2816]{5,4,0,3,1,2:T(8,128)} %bitcast.48) | data formatting | bytes 17301504 | tf_op jit(solution)/shard_map/transpose | solution.py:71
  206.7 10.0 %reshape.363 = f32[768,2816]{1,0:T(8,128)} reshape(f32[2,8,4,2,6,2816]{5,4,3,2,1,0:T(8,128)} %copy.17) | data formatting | bytes 17301504 | tf_op jit(solution)/shard_map/reshape | solution.py:71
  216.8 3.8 dynamic-slice_convert_fusion.1
  222.1 7.7 %convolution_multiply_fusion = f32[2816,768]{1,0:T(8,128)} fusion(bf16[512,2816]{1,0:T(8,128)(2,1)} %get-tuple-element.156, bf16[512,768]{1,0:T(8,128)(2,1)S(1)} %bitcast.62), kind=kOutput, calls=%fused_computation.43 | convolution fusion | flops 2216755200 | bytes 12320768 | tf_op jit(solution)/shard_map/dot_general | solution.py:172
  229.8 9.5 %reshape.364 = f32[4,8,2,2,22,768]{5,4,3,2,1,0:T(8,128)} reshape(f32[2816,768]{1,0:T(8,128)} %convolution_multiply_fusion) | data formatting | bytes 17301504 | tf_op jit(solution)/shard_map/reshape | solution.py:70
  239.3 8.8 %copy.18 = f32[2,8,4,2,22,768]{5,4,3,2,1,0:T(8,128)} copy(f32[2,8,4,2,22,768]{5,4,0,3,1,2:T(8,128)} %bitcast.49) | data formatting | bytes 17301504 | tf_op jit(solution)/shard_map/transpose | solution.py:71
  248.0 9.5 %reshape.365 = f32[2816,768]{1,0:T(8,128)} reshape(f32[2,8,4,2,22,768]{5,4,3,2,1,0:T(8,128)} %copy.18) | data formatting | bytes 17301504 | tf_op jit(solution)/shard_map/reshape | solution.py:71
  257.5 2.6 dynamic-slice_convert_fusion
  260.7 5.8 %collective-permute-start.26 = (bf16[1,3,32,768]{3,2,1,0:T(8,128)(2,1)S(1)}, bf16[1,3,32,768]{3,2,1,0:T(8,128)(2,1)S(1)}, u32[]{:S(2)}, u32[]{:S(2)}) collective-permute-start(bf16[1,3,32,768]{3,2,1,0:T(8,128)(2,1)S(1)} %get-tuple-element.138), channel_id=1, source_target_pairs={{0,1},{2,3},{4,5},{6,7},{8,9},{10,11},{12,13},{14,15},{16,17},{18,... | collective-permute-start | bytes 442376 | tf_op jit(solution)/shard_map/ppermute | solution.py:82
  267.9 5.7 %fusion.103 = bf16[1,16,32,768]{3,2,1,0:T(8,128)(2,1)} fusion(bf16[1,16,32,768]{3,2,1,0:T(8,128)(2,1)S(1)} %copy-done.1, bf16[16,32,2816]{2,1,0:T(8,128)(2,1)S(1)} %bitcast.65, bf16[2816,768,1]{1,0,2:T(8,128)(2,1)} %bitcast.58), kind=kOutput, calls=%fused_computation.255 | convolution fusion | flops 2215772160 | bytes 8781824 | tf_op jit(solution)/shard_map/dot_general | solution.py:176
  280.4 3.0 collective-permute-start.59
  287.3 3.9 collective-permute-start.60
  291.3 2.9 collective-permute-start.38
  294.3 3.7 collective-permute-start.61
  298.1 2.5 collective-permute-done.30
  325.2 2.8 collective-permute-done.56
  335.4 2.6 collective-permute-done.35
  344.0 3.1 collective-permute-start.47
  349.3 3.4 collective-permute-start.48
  353.2 3.6 collective-permute-start.71
  358.1 3.9 collective-permute-done.67
  364.7 2.4 collective-permute-done.68
  374.0 12.6 %fusion.194 = bf16[1,16,32,768]{3,2,1,0:T(8,128)(2,1)} fusion(f32[1,22,32,768]{3,2,1,0:T(8,128)S(1)} %maximum_convert_fusion, f32[768]{0:T(1024)S(1)} %copy-done.83, f32[768]{0:T(1024)S(1)} %copy-done.85, f32[768]{0:T(1024)S(1)} %get-tuple-element.58, f32[768]{0:T(1024)S(1)} %get-tuple-element.59, f32[768]{0:T(1024)S(1)} %get-tuple-element.60, ...), kind=kLoop, calls=%fused_computation.346 | loop fusion | flops 40108032 | bytes 14948352 | tf_op jit(solution)/shard_map/convert_element_type | solution.py:204
  387.9 79.2 %all-reduce.4.cloned.1.call-done = f32[7,7,768]{2,1,0:T(8,128)} async-done(((f32[7,7,768]{2,1,0:T(8,128)}), f32[7,7,768]{2,1,0:T(8,128)}) %all-reduce.4.cloned.1.call-update) | async-done | bytes 150544 | tf_op jit(solution)/shard_map/psum | solution.py:193
  (475 shorter events, 98.1 us)
Async XLA Ops:
  7.2 460.0 %all-reduce.4.cloned.1.call-start = ((), (), s32[]{:S(2)}) async-start(), calls=%async_computation | async-start | bytes 344064 | tf_op jit(solution)/shard_map/psum | solution.py:193
  7.2 12.3 %collective-permute-start.14 = (bf16[22,768]{1,0:T(8,128)(2,1)}, bf16[22,768]{1,0:T(8,128)(2,1)S(1)}, u32[]{:S(2)}, u32[]{:S(2)}) collective-permute-start(bf16[22,768]{1,0:T(8,128)(2,1)} %param.10), channel_id=1, source_target_pairs={{0,2},{2,0},{1,3},{3,1},{4,6},{6,4},{5,7},{7,5},{8,10},{10,8},{9,1... | collective-permute-start | bytes 101384 | tf_op jit(solution)/shard_map/ppermute | solution.py:27
  7.3 14.1 %collective-permute-start.2 = (bf16[6,2816]{1,0:T(8,128)(2,1)}, bf16[6,2816]{1,0:T(8,128)(2,1)S(1)}, u32[]{:S(2)}, u32[]{:S(2)}) collective-permute-start(bf16[6,2816]{1,0:T(8,128)(2,1)} %param.9), channel_id=1, source_target_pairs={{0,2},{2,0},{1,3},{3,1},{4,6},{6,4},{5,7},{7,5},{8,10},{10,8},{9,1... | collective-permute-start | bytes 101384 | tf_op jit(solution)/shard_map/ppermute | solution.py:27
  11.1 21.9 %collective-permute-start = (bf16[1,3,32,768]{3,2,1,0:T(8,128)(2,1)S(1)}, bf16[1,3,32,768]{3,2,1,0:T(8,128)(2,1)S(1)}, u32[]{:S(2)}, u32[]{:S(2)}) collective-permute-start(bf16[1,3,32,768]{3,2,1,0:T(8,128)(2,1)S(1)} %get-tuple-element.140), channel_id=1, source_target_pairs={{0,1},{2,3},{4,5},{6,7},{8,9},{10,11},{12,13},{14,15},{16,17},{18,... | collective-permute-start | bytes 442376 | tf_op jit(solution)/shard_map/ppermute | solution.py:82
  15.3 18.0 %collective-permute-start.1 = (bf16[1,3,32,768]{3,2,1,0:T(8,128)(2,1)S(1)}, bf16[1,3,32,768]{3,2,1,0:T(8,128)(2,1)S(1)}, u32[]{:S(2)}, u32[]{:S(2)}) collective-permute-start(bf16[1,3,32,768]{3,2,1,0:T(8,128)(2,1)S(1)} %get-tuple-element.141), channel_id=1, source_target_pairs={{1,0},{3,2},{5,4},{7,6},{9,8},{11,10},{13,12},{15,14},{17,16},{19,... | collective-permute-start | bytes 442376 | tf_op jit(solution)/shard_map/ppermute | solution.py:85
  25.4 31.6 %collective-permute-start.18 = (bf16[88,768]{1,0:T(8,128)(2,1)S(1)}, bf16[88,768]{1,0:T(8,128)(2,1)}, u32[]{:S(2)}, u32[]{:S(2)}) collective-permute-start(bf16[88,768]{1,0:T(8,128)(2,1)S(1)} %dynamic_update_slice.115), channel_id=1, source_target_pairs={{0,192},{64,0},{128,64},{192,128},{1,193},{65,1},{129,65},{193,129... | collective-permute-start | bytes 405512 | tf_op jit(solution)/shard_map/ppermute | solution.py:31
  28.5 22.0 %collective-permute-start.16 = (bf16[88,768]{1,0:T(8,128)(2,1)S(1)}, bf16[88,768]{1,0:T(8,128)(2,1)}, u32[]{:S(2)}, u32[]{:S(2)}) collective-permute-start(bf16[88,768]{1,0:T(8,128)(2,1)S(1)} %dynamic_update_slice.115), channel_id=1, source_target_pairs={{0,64},{64,128},{128,192},{192,0},{1,65},{65,129},{129,193},{193,1... | collective-permute-start | bytes 405512 | tf_op jit(solution)/shard_map/ppermute | solution.py:27
  29.2 30.8 %collective-permute-start.6 = (bf16[24,2816]{1,0:T(8,128)(2,1)S(1)}, bf16[24,2816]{1,0:T(8,128)(2,1)S(1)}, u32[]{:S(2)}, u32[]{:S(2)}) collective-permute-start(bf16[24,2816]{1,0:T(8,128)(2,1)S(1)} %dynamic_update_slice.99), channel_id=1, source_target_pairs={{0,192},{64,0},{128,64},{192,128},{1,193},{65,1},{129,65},{193,129... | collective-permute-start | bytes 405512 | tf_op jit(solution)/shard_map/ppermute | solution.py:31
  33.0 17.6 %collective-permute-start.4 = (bf16[24,2816]{1,0:T(8,128)(2,1)S(1)}, bf16[24,2816]{1,0:T(8,128)(2,1)S(1)}, u32[]{:S(2)}, u32[]{:S(2)}) collective-permute-start(bf16[24,2816]{1,0:T(8,128)(2,1)S(1)} %dynamic_update_slice.99), channel_id=1, source_target_pairs={{0,64},{64,128},{128,192},{192,0},{1,65},{65,129},{129,193},{193,1... | collective-permute-start | bytes 405512 | tf_op jit(solution)/shard_map/ppermute | solution.py:27
  50.6 9.4 %collective-permute-start.5 = (bf16[24,2816]{1,0:T(8,128)(2,1)S(1)}, bf16[24,2816]{1,0:T(8,128)(2,1)S(1)}, u32[]{:S(2)}, u32[]{:S(2)}) collective-permute-start(bf16[24,2816]{1,0:T(8,128)(2,1)S(1)} %collective-permute-done.4), channel_id=1, source_target_pairs={{0,64},{64,128},{128,192},{192,0},{1,65},{65,129},{129,193},{193,1... | collective-permute-start | bytes 405512 | tf_op jit(solution)/shard_map/ppermute | solution.py:27
  58.0 19.1 %collective-permute-start.19 = (bf16[352,768]{1,0:T(8,128)(2,1)S(1)}, bf16[352,768]{1,0:T(8,128)(2,1)S(1)}, u32[]{:S(2)}, u32[]{:S(2)}) collective-permute-start(bf16[352,768]{1,0:T(8,128)(2,1)S(1)} %constant_dynamic-update-slice_fusion.8), channel_id=1, source_target_pairs={{0,8},{8,16},{16,24},{24,32},{32,40},{40,48},{48,56},{56,0},{1,9},... | collective-permute-start | bytes 1622024 | tf_op jit(solution)/shard_map/ppermute | solution.py:27
  60.0 28.7 %collective-permute-start.7 = (bf16[96,2816]{1,0:T(8,128)(2,1)S(1)}, bf16[96,2816]{1,0:T(8,128)(2,1)S(1)}, u32[]{:S(2)}, u32[]{:S(2)}) collective-permute-start(bf16[96,2816]{1,0:T(8,128)(2,1)S(1)} %constant_dynamic-update-slice_fusion.20), channel_id=1, source_target_pairs={{0,8},{8,16},{16,24},{24,32},{32,40},{40,48},{48,56},{56,0},{1,9},... | collective-permute-start | bytes 1622024 | tf_op jit(solution)/shard_map/ppermute | solution.py:27
  62.3 26.7 %collective-permute-start.11 = (bf16[96,2816]{1,0:T(8,128)(2,1)S(1)}, bf16[96,2816]{1,0:T(8,128)(2,1)S(1)}, u32[]{:S(2)}, u32[]{:S(2)}) collective-permute-start(bf16[96,2816]{1,0:T(8,128)(2,1)S(1)} %constant_dynamic-update-slice_fusion.20), channel_id=1, source_target_pairs={{0,56},{8,0},{16,8},{24,16},{32,24},{40,32},{48,40},{56,48},{1,57}... | collective-permute-start | bytes 1622024 | tf_op jit(solution)/shard_map/ppermute | solution.py:31
  64.9 27.9 %collective-permute-start.23 = (bf16[352,768]{1,0:T(8,128)(2,1)S(1)}, bf16[352,768]{1,0:T(8,128)(2,1)S(1)}, u32[]{:S(2)}, u32[]{:S(2)}) collective-permute-start(bf16[352,768]{1,0:T(8,128)(2,1)S(1)} %constant_dynamic-update-slice_fusion.8), channel_id=1, source_target_pairs={{0,56},{8,0},{16,8},{24,16},{32,24},{40,32},{48,40},{56,48},{1,57}... | collective-permute-start | bytes 1622024 | tf_op jit(solution)/shard_map/ppermute | solution.py:31
  77.1 23.2 %collective-permute-start.20 = (bf16[352,768]{1,0:T(8,128)(2,1)S(1)}, bf16[352,768]{1,0:T(8,128)(2,1)S(1)}, u32[]{:S(2)}, u32[]{:S(2)}) collective-permute-start(bf16[352,768]{1,0:T(8,128)(2,1)S(1)} %collective-permute-done.19), channel_id=1, source_target_pairs={{0,8},{8,16},{16,24},{24,32},{32,40},{40,48},{48,56},{56,0},{1,9},... | collective-permute-start | bytes 1622024 | tf_op jit(solution)/shard_map/ppermute | solution.py:27
  88.7 23.2 %collective-permute-start.8 = (bf16[96,2816]{1,0:T(8,128)(2,1)S(1)}, bf16[96,2816]{1,0:T(8,128)(2,1)S(1)}, u32[]{:S(2)}, u32[]{:S(2)}) collective-permute-start(bf16[96,2816]{1,0:T(8,128)(2,1)S(1)} %collective-permute-done.7), channel_id=1, source_target_pairs={{0,8},{8,16},{16,24},{24,32},{32,40},{40,48},{48,56},{56,0},{1,9},... | collective-permute-start | bytes 1622024 | tf_op jit(solution)/shard_map/ppermute | solution.py:27
  89.0 22.9 %collective-permute-start.12 = (bf16[96,2816]{1,0:T(8,128)(2,1)S(1)}, bf16[96,2816]{1,0:T(8,128)(2,1)S(1)}, u32[]{:S(2)}, u32[]{:S(2)}) collective-permute-start(bf16[96,2816]{1,0:T(8,128)(2,1)S(1)} %collective-permute-done.11), channel_id=1, source_target_pairs={{0,56},{8,0},{16,8},{24,16},{32,24},{40,32},{48,40},{56,48},{1,57}... | collective-permute-start | bytes 1622024 | tf_op jit(solution)/shard_map/ppermute | solution.py:31
  92.8 22.5 %collective-permute-start.24 = (bf16[352,768]{1,0:T(8,128)(2,1)S(1)}, bf16[352,768]{1,0:T(8,128)(2,1)S(1)}, u32[]{:S(2)}, u32[]{:S(2)}) collective-permute-start(bf16[352,768]{1,0:T(8,128)(2,1)S(1)} %collective-permute-done.23), channel_id=1, source_target_pairs={{0,56},{8,0},{16,8},{24,16},{32,24},{40,32},{48,40},{56,48},{1,57}... | collective-permute-start | bytes 1622024 | tf_op jit(solution)/shard_map/ppermute | solution.py:31
  100.3 23.2 %collective-permute-start.21 = (bf16[352,768]{1,0:T(8,128)(2,1)S(1)}, bf16[352,768]{1,0:T(8,128)(2,1)S(1)}, u32[]{:S(2)}, u32[]{:S(2)}) collective-permute-start(bf16[352,768]{1,0:T(8,128)(2,1)S(1)} %collective-permute-done.20), channel_id=1, source_target_pairs={{0,8},{8,16},{16,24},{24,32},{32,40},{40,48},{48,56},{56,0},{1,9},... | collective-permute-start | bytes 1622024 | tf_op jit(solution)/shard_map/ppermute | solution.py:27
  111.9 23.2 %collective-permute-start.9 = (bf16[96,2816]{1,0:T(8,128)(2,1)S(1)}, bf16[96,2816]{1,0:T(8,128)(2,1)S(1)}, u32[]{:S(2)}, u32[]{:S(2)}) collective-permute-start(bf16[96,2816]{1,0:T(8,128)(2,1)S(1)} %collective-permute-done.8), channel_id=1, source_target_pairs={{0,8},{8,16},{16,24},{24,32},{32,40},{40,48},{48,56},{56,0},{1,9},... | collective-permute-start | bytes 1622024 | tf_op jit(solution)/shard_map/ppermute | solution.py:27
  111.9 42.5 %collective-permute-start.13 = (bf16[96,2816]{1,0:T(8,128)(2,1)S(1)}, bf16[96,2816]{1,0:T(8,128)(2,1)S(1)}, u32[]{:S(2)}, u32[]{:S(2)}) collective-permute-start(bf16[96,2816]{1,0:T(8,128)(2,1)S(1)} %collective-permute-done.12), channel_id=1, source_target_pairs={{0,56},{8,0},{16,8},{24,16},{32,24},{40,32},{48,40},{56,48},{1,57}... | collective-permute-start | bytes 1622024 | tf_op jit(solution)/shard_map/ppermute | solution.py:31
  115.2 31.5 %collective-permute-start.25 = (bf16[352,768]{1,0:T(8,128)(2,1)S(1)}, bf16[352,768]{1,0:T(8,128)(2,1)S(1)}, u32[]{:S(2)}, u32[]{:S(2)}) collective-permute-start(bf16[352,768]{1,0:T(8,128)(2,1)S(1)} %collective-permute-done.24), channel_id=1, source_target_pairs={{0,56},{8,0},{16,8},{24,16},{32,24},{40,32},{48,40},{56,48},{1,57}... | collective-permute-start | bytes 1622024 | tf_op jit(solution)/shard_map/ppermute | solution.py:31
  123.4 23.2 %collective-permute-start.22 = (bf16[352,768]{1,0:T(8,128)(2,1)S(1)}, bf16[352,768]{1,0:T(8,128)(2,1)S(1)}, u32[]{:S(2)}, u32[]{:S(2)}) collective-permute-start(bf16[352,768]{1,0:T(8,128)(2,1)S(1)} %collective-permute-done.21), channel_id=1, source_target_pairs={{0,8},{8,16},{16,24},{24,32},{32,40},{40,48},{48,56},{56,0},{1,9},... | collective-permute-start | bytes 1622024 | tf_op jit(solution)/shard_map/ppermute | solution.py:27
  135.0 19.2 %collective-permute-start.10 = (bf16[96,2816]{1,0:T(8,128)(2,1)S(1)}, bf16[96,2816]{1,0:T(8,128)(2,1)S(1)}, u32[]{:S(2)}, u32[]{:S(2)}) collective-permute-start(bf16[96,2816]{1,0:T(8,128)(2,1)S(1)} %collective-permute-done.9), channel_id=1, source_target_pairs={{0,8},{8,16},{16,24},{24,32},{32,40},{40,48},{48,56},{56,0},{1,9},... | collective-permute-start | bytes 1622024 | tf_op jit(solution)/shard_map/ppermute | solution.py:27
  220.6 55.1 %collective-permute-start.28 = (bf16[384,2816]{1,0:T(8,128)(2,1)}, bf16[384,2816]{1,0:T(8,128)(2,1)}, u32[]{:S(2)}, u32[]{:S(2)}) collective-permute-start(bf16[384,2816]{1,0:T(8,128)(2,1)} %dynamic-slice_convert_fusion.1), channel_id=1, source_target_pairs={{0,2},{2,0},{1,3},{3,1},{4,6},{6,4},{5,7},{7,5},{8,10},{10,8},{9,1... | collective-permute-start | bytes 6488072 | tf_op jit(solution)/shard_map/ppermute | solution.py:45
  260.1 19.8 %collective-permute-start.51 = (bf16[1408,768]{1,0:T(8,128)(2,1)S(1)}, bf16[1408,768]{1,0:T(8,128)(2,1)S(1)}, u32[]{:S(2)}, u32[]{:S(2)}) collective-permute-start(bf16[1408,768]{1,0:T(8,128)(2,1)S(1)} %dynamic-slice_convert_fusion), channel_id=1, source_target_pairs={{0,2},{2,0},{1,3},{3,1},{4,6},{6,4},{5,7},{7,5},{8,10},{10,8},{9,1... | collective-permute-start | bytes 6488072 | tf_op jit(solution)/shard_map/ppermute | solution.py:45
  260.7 12.9 %collective-permute-start.26 = (bf16[1,3,32,768]{3,2,1,0:T(8,128)(2,1)S(1)}, bf16[1,3,32,768]{3,2,1,0:T(8,128)(2,1)S(1)}, u32[]{:S(2)}, u32[]{:S(2)}) collective-permute-start(bf16[1,3,32,768]{3,2,1,0:T(8,128)(2,1)S(1)} %get-tuple-element.138), channel_id=1, source_target_pairs={{0,1},{2,3},{4,5},{6,7},{8,9},{10,11},{12,13},{14,15},{16,17},{18,... | collective-permute-start | bytes 442376 | tf_op jit(solution)/shard_map/ppermute | solution.py:82
  266.6 8.9 %collective-permute-start.27 = (bf16[1,3,32,768]{3,2,1,0:T(8,128)(2,1)S(1)}, bf16[1,3,32,768]{3,2,1,0:T(8,128)(2,1)S(1)}, u32[]{:S(2)}, u32[]{:S(2)}) collective-permute-start(bf16[1,3,32,768]{3,2,1,0:T(8,128)(2,1)S(1)} %get-tuple-element.139), channel_id=1, source_target_pairs={{1,0},{3,2},{5,4},{7,6},{9,8},{11,10},{13,12},{15,14},{17,16},{19,... | collective-permute-start | bytes 442376 | tf_op jit(solution)/shard_map/ppermute | solution.py:85
  279.6 11.6 %collective-permute-start.29 = (bf16[48,1408]{1,0:T(8,128)(2,1)S(1)}, bf16[48,1408]{1,0:T(8,128)(2,1)S(1)}, u32[]{:S(2)}, u32[]{:S(2)}) collective-permute-start(bf16[48,1408]{1,0:T(8,128)(2,1)S(1)} %get-tuple-element.136), channel_id=1, source_target_pairs={{0,8},{8,16},{16,24},{24,32},{32,40},{40,48},{48,56},{56,0},{1,9},... | collective-permute-start | bytes 405512 | tf_op jit(solution)/shard_map/ppermute | solution.py:51
  280.4 6.8 %collective-permute-start.59 = (bf16[176,384]{1,0:T(8,128)(2,1)S(1)}, bf16[176,384]{1,0:T(8,128)(2,1)S(1)}, u32[]{:S(2)}, u32[]{:S(2)}) collective-permute-start(bf16[176,384]{1,0:T(8,128)(2,1)S(1)} %get-tuple-element.121), channel_id=1, source_target_pairs={{0,56},{8,0},{16,8},{24,16},{32,24},{40,32},{48,40},{56,48},{1,57}... | collective-permute-start | bytes 405512 | tf_op jit(solution)/shard_map/ppermute | solution.py:52
  283.4 10.8 %collective-permute-start.52 = (bf16[176,384]{1,0:T(8,128)(2,1)S(1)}, bf16[176,384]{1,0:T(8,128)(2,1)S(1)}, u32[]{:S(2)}, u32[]{:S(2)}) collective-permute-start(bf16[176,384]{1,0:T(8,128)(2,1)S(1)} %get-tuple-element.122), channel_id=1, source_target_pairs={{0,8},{8,16},{16,24},{24,32},{32,40},{40,48},{48,56},{56,0},{1,9},... | collective-permute-start | bytes 405512 | tf_op jit(solution)/shard_map/ppermute | solution.py:51
  284.4 6.8 %collective-permute-start.37 = (bf16[48,1408]{1,0:T(8,128)(2,1)S(1)}, bf16[48,1408]{1,0:T(8,128)(2,1)S(1)}, u32[]{:S(2)}, u32[]{:S(2)}) collective-permute-start(bf16[48,1408]{1,0:T(8,128)(2,1)S(1)} %fusion.226), channel_id=1, source_target_pairs={{0,56},{8,0},{16,8},{24,16},{32,24},{40,32},{48,40},{56,48},{1,57}... | collective-permute-start | bytes 405512 | tf_op jit(solution)/shard_map/ppermute | solution.py:52
  287.3 7.0 %collective-permute-start.60 = (bf16[176,384]{1,0:T(8,128)(2,1)S(1)}, bf16[176,384]{1,0:T(8,128)(2,1)S(1)}, u32[]{:S(2)}, u32[]{:S(2)}) collective-permute-start(bf16[176,384]{1,0:T(8,128)(2,1)S(1)} %fusion.214), channel_id=1, source_target_pairs={{0,56},{8,0},{16,8},{24,16},{32,24},{40,32},{48,40},{56,48},{1,57}... | collective-permute-start | bytes 405512 | tf_op jit(solution)/shard_map/ppermute | solution.py:52
  294.3 8.4 %collective-permute-start.61 = (bf16[176,384]{1,0:T(8,128)(2,1)S(1)}, bf16[176,384]{1,0:T(8,128)(2,1)S(1)}, u32[]{:S(2)}, u32[]{:S(2)}) collective-permute-start(bf16[176,384]{1,0:T(8,128)(2,1)S(1)} %get-tuple-element.119), channel_id=1, source_target_pairs={{0,56},{8,0},{16,8},{24,16},{32,24},{40,32},{48,40},{56,48},{1,57}... | collective-permute-start | bytes 405512 | tf_op jit(solution)/shard_map/ppermute | solution.py:52
  298.1 6.9 %collective-permute-start.53 = (bf16[176,384]{1,0:T(8,128)(2,1)S(1)}, bf16[176,384]{1,0:T(8,128)(2,1)S(1)}, u32[]{:S(2)}, u32[]{:S(2)}) collective-permute-start(bf16[176,384]{1,0:T(8,128)(2,1)S(1)} %get-tuple-element.120), channel_id=1, source_target_pairs={{0,8},{8,16},{16,24},{24,32},{32,40},{40,48},{48,56},{56,0},{1,9},... | collective-permute-start | bytes 405512 | tf_op jit(solution)/shard_map/ppermute | solution.py:51
  301.5 7.4 %collective-permute-start.31 = (bf16[48,1408]{1,0:T(8,128)(2,1)S(1)}, bf16[48,1408]{1,0:T(8,128)(2,1)S(1)}, u32[]{:S(2)}, u32[]{:S(2)}) collective-permute-start(bf16[48,1408]{1,0:T(8,128)(2,1)S(1)} %get-tuple-element.132), channel_id=1, source_target_pairs={{0,8},{8,16},{16,24},{24,32},{32,40},{40,48},{48,56},{56,0},{1,9},... | collective-permute-start | bytes 405512 | tf_op jit(solution)/shard_map/ppermute | solution.py:51
  305.1 7.7 %collective-permute-start.54 = (bf16[176,384]{1,0:T(8,128)(2,1)S(1)}, bf16[176,384]{1,0:T(8,128)(2,1)S(1)}, u32[]{:S(2)}, u32[]{:S(2)}) collective-permute-start(bf16[176,384]{1,0:T(8,128)(2,1)S(1)} %get-tuple-element.118), channel_id=1, source_target_pairs={{0,8},{8,16},{16,24},{24,32},{32,40},{40,48},{48,56},{56,0},{1,9},... | collective-permute-start | bytes 405512 | tf_op jit(solution)/shard_map/ppermute | solution.py:51
  309.1 7.0 %collective-permute-start.32 = (bf16[48,1408]{1,0:T(8,128)(2,1)S(1)}, bf16[48,1408]{1,0:T(8,128)(2,1)S(1)}, u32[]{:S(2)}, u32[]{:S(2)}) collective-permute-start(bf16[48,1408]{1,0:T(8,128)(2,1)S(1)} %get-tuple-element.130), channel_id=1, source_target_pairs={{0,8},{8,16},{16,24},{24,32},{32,40},{40,48},{48,56},{56,0},{1,9},... | collective-permute-start | bytes 405512 | tf_op jit(solution)/shard_map/ppermute | solution.py:51
  313.0 7.0 %collective-permute-start.55 = (bf16[176,384]{1,0:T(8,128)(2,1)S(1)}, bf16[176,384]{1,0:T(8,128)(2,1)S(1)}, u32[]{:S(2)}, u32[]{:S(2)}) collective-permute-start(bf16[176,384]{1,0:T(8,128)(2,1)S(1)} %get-tuple-element.116), channel_id=1, source_target_pairs={{0,8},{8,16},{16,24},{24,32},{32,40},{40,48},{48,56},{56,0},{1,9},... | collective-permute-start | bytes 405512 | tf_op jit(solution)/shard_map/ppermute | solution.py:51
  320.4 7.6 %collective-permute-start.56 = (bf16[176,384]{1,0:T(8,128)(2,1)S(1)}, bf16[176,384]{1,0:T(8,128)(2,1)S(1)}, u32[]{:S(2)}, u32[]{:S(2)}) collective-permute-start(bf16[176,384]{1,0:T(8,128)(2,1)S(1)} %get-tuple-element.114), channel_id=1, source_target_pairs={{0,8},{8,16},{16,24},{24,32},{32,40},{40,48},{48,56},{56,0},{1,9},... | collective-permute-start | bytes 405512 | tf_op jit(solution)/shard_map/ppermute | solution.py:51
  323.0 7.2 %collective-permute-start.42 = (bf16[48,1408]{1,0:T(8,128)(2,1)S(1)}, bf16[48,1408]{1,0:T(8,128)(2,1)S(1)}, u32[]{:S(2)}, u32[]{:S(2)}) collective-permute-start(bf16[48,1408]{1,0:T(8,128)(2,1)S(1)} %get-tuple-element.125), channel_id=1, source_target_pairs={{0,56},{8,0},{16,8},{24,16},{32,24},{40,32},{48,40},{56,48},{1,57}... | collective-permute-start | bytes 405512 | tf_op jit(solution)/shard_map/ppermute | solution.py:52
  324.0 7.6 %collective-permute-start.34 = (bf16[48,1408]{1,0:T(8,128)(2,1)S(1)}, bf16[48,1408]{1,0:T(8,128)(2,1)S(1)}, u32[]{:S(2)}, u32[]{:S(2)}) collective-permute-start(bf16[48,1408]{1,0:T(8,128)(2,1)S(1)} %get-tuple-element.126), channel_id=1, source_target_pairs={{0,8},{8,16},{16,24},{24,32},{32,40},{40,48},{48,56},{56,0},{1,9},... | collective-permute-start | bytes 405512 | tf_op jit(solution)/shard_map/ppermute | solution.py:51
  340.2 8.9 %collective-permute-start.43 = (bf16[12,1408]{1,0:T(8,128)(2,1)S(1)}, bf16[12,1408]{1,0:T(8,128)(2,1)S(1)}, u32[]{:S(2)}, u32[]{:S(2)}) collective-permute-start(bf16[12,1408]{1,0:T(8,128)(2,1)S(1)} %get-tuple-element.149), channel_id=1, source_target_pairs={{0,64},{64,128},{128,192},{192,0},{1,65},{65,129},{129,193},{193,1... | collective-permute-start | bytes 101384 | tf_op jit(solution)/shard_map/ppermute | solution.py:51
  343.7 9.0 %collective-permute-start.66 = (bf16[44,384]{1,0:T(8,128)(2,1)S(1)}, bf16[44,384]{1,0:T(8,128)(2,1)S(1)}, u32[]{:S(2)}, u32[]{:S(2)}) collective-permute-start(bf16[44,384]{1,0:T(8,128)(2,1)S(1)} %get-tuple-element.145), channel_id=1, source_target_pairs={{0,64},{64,128},{128,192},{192,0},{1,65},{65,129},{129,193},{193,1... | collective-permute-start | bytes 101384 | tf_op jit(solution)/shard_map/ppermute | solution.py:51
  349.3 12.8 %collective-permute-start.48 = (bf16[12,1408]{1,0:T(8,128)(2,1)S(1)}, bf16[12,1408]{1,0:T(8,128)(2,1)S(1)}, u32[]{:S(2)}, u32[]{:S(2)}) collective-permute-start(bf16[12,1408]{1,0:T(8,128)(2,1)S(1)} %get-tuple-element.146), channel_id=1, source_target_pairs={{0,192},{64,0},{128,64},{192,128},{1,193},{65,1},{129,65},{193,129... | collective-permute-start | bytes 101384 | tf_op jit(solution)/shard_map/ppermute | solution.py:52
  353.2 11.6 %collective-permute-start.71 = (bf16[44,384]{1,0:T(8,128)(2,1)S(1)}, bf16[44,384]{1,0:T(8,128)(2,1)S(1)}, u32[]{:S(2)}, u32[]{:S(2)}) collective-permute-start(bf16[44,384]{1,0:T(8,128)(2,1)S(1)} %get-tuple-element.142), channel_id=1, source_target_pairs={{0,192},{64,0},{128,64},{192,128},{1,193},{65,1},{129,65},{193,129... | collective-permute-start | bytes 101384 | tf_op jit(solution)/shard_map/ppermute | solution.py:52
  368.7 18.0 %collective-permute-start.50 = (f32[6,2816]{1,0:T(8,128)S(1)}, f32[6,2816]{1,0:T(8,128)S(1)}, u32[]{:S(2)}, u32[]{:S(2)}) collective-permute-start(f32[6,2816]{1,0:T(8,128)S(1)} %fusion.238), channel_id=1, source_target_pairs={{0,1},{1,0},{2,3},{3,2},{4,5},{5,4},{6,7},{7,6},{8,9},{9,8},{10,11... | collective-permute-start | bytes 202760 | tf_op jit(solution)/shard_map/ppermute | solution.py:74
  371.3 16.0 %collective-permute-start.73 = (f32[22,768]{1,0:T(8,128)S(1)}, f32[22,768]{1,0:T(8,128)S(1)}, u32[]{:S(2)}, u32[]{:S(2)}) collective-permute-start(f32[22,768]{1,0:T(8,128)S(1)} %fusion.258), channel_id=1, source_target_pairs={{0,1},{1,0},{2,3},{3,2},{4,5},{5,4},{6,7},{7,6},{8,9},{9,8},{10,11... | collective-permute-start | bytes 202760 | tf_op jit(solution)/shard_map/ppermute | solution.py:74
  (120 other events, 1233.2 us)
Sparse Core Ops, SparseCore 0:
  222.2 244.9 all-reduce.3
